TPU v7x, 512 devices: a whole 4x4x16 slice. The times are simulated.
512 devices in a mesh: dp: 32 (over x, y, core), expert: 16 (over z).
Axes of the slice: x: 4, y: 4, z: 16, core: 2. Of those that a mesh axis runs over, the one named last changes fastest.
Arguments:
- out_grad: bfloat16 [65536, 2048], P(('dp', 'expert')), may hold values from -6 to 6
- expert_ids: int32 [65536, 4], P(('dp', 'expert')), may hold values from 0 to 15, all different within a row; in each aligned block of 128 rows (0 to 127, 128 to 255, ...) at most 64 rows name the same one
- route_weights: bfloat16 [65536, 4], P(('dp', 'expert')), may hold values from 0.049804688 to 1
- pre_activations: bfloat16 [65536, 4, 1536], P(('dp', 'expert')), may hold values from -6 to 6
- down_weight: bfloat16 [16, 768, 2048], P('expert', 'dp'), may hold values from -0.21875 to 0.21875
Outputs:
- pre_grad: bfloat16 [65536, 4, 1536], P(('dp', 'expert'))
- weight_grad: bfloat16 [65536, 4], P(('dp', 'expert'))
- down_grad: bfloat16 [16, 768, 2048], P('expert', 'dp')
Inputs may be any that keep to these rules, and one draw needn't show every extreme that they name: `expert_ids`: among the 128 rows of one device, each expert is named by at most 64 rows, a bound that some block reaches; the numbers in a row are distinct.
All inputs are finite; a program needn't handle non-finite values.
Results may differ from a plain program's by a relative error of at most 0.015.
Values may be sent and summed in bfloat16 or wider, within the bound.
No kernel may reach another device: no remote copies, remote signals or barrier semaphores. Data moves between devices by JAX's collectives and lax.ppermute only.
A program may use at most 64 MiB of HBM per device.

v0:
```python
import jax
import jax.numpy as jnp
from jax import lax
from jax.sharding import PartitionSpec as P

F32 = jnp.float32
BF16 = jnp.bfloat16


def gather_rows(x):
    return lax.all_gather(x, "dp", axis=0, tiled=True)


def body(out_grad, expert_ids, route_weights, pre_activations, down_weight):
    tok, width = out_grad.shape
    top = expert_ids.shape[1]
    units = pre_activations.shape[2] // 2
    ndp = lax.axis_size("dp")
    rows = down_weight.shape[1]
    n_all = ndp * tok
    w_all = lax.all_gather(down_weight, "expert", axis=0, tiled=True)
    experts = w_all.shape[0]
    wcat = w_all.reshape(experts * rows, width)
    og_all = gather_rows(out_grad)
    ids_t = gather_rows(expert_ids).T
    rw_t = gather_rows(route_weights).T.astype(F32)
    gate = pre_activations[..., :units].astype(F32)
    up = pre_activations[..., units:].astype(F32)
    sig = jax.nn.sigmoid(gate)
    hidden = (gate * sig * up).astype(BF16)
    send_h = hidden.reshape(tok, top, ndp, rows).transpose(2, 0, 1, 3)
    got_h = lax.all_to_all(send_h, "dp", 0, 0, tiled=True)
    hid_t = got_h.transpose(2, 3, 0, 1).reshape(top, rows, n_all).astype(F32)
    eidx = jnp.arange(experts, dtype=jnp.int32)[:, None, None]
    hp = jnp.zeros((experts, rows, n_all), F32)
    for k in range(top):
        hp = hp + jnp.where(
            ids_t[k][None, None, :] == eidx, (rw_t[k][None, :] * hid_t[k])[None], 0.0
        )
    hp = hp.reshape(experts * rows, n_all).astype(BF16)
    part = lax.dot_general(hp, og_all, (((1,), (0,)), ((), ())), preferred_element_type=F32)
    r_t = lax.dot_general(wcat, og_all, (((1,), (1,)), ((), ())), preferred_element_type=F32)
    r_t = r_t.reshape(experts, rows, n_all)
    hg_t = jnp.stack(
        [jnp.sum(jnp.where(ids_t[k][None, None, :] == eidx, r_t, 0.0), axis=0) for k in range(top)]
    ).astype(BF16)
    send_g = hg_t.reshape(top, rows, ndp, tok).transpose(2, 3, 0, 1)
    got_g = lax.all_to_all(send_g, "dp", 0, 0, tiled=True)
    hidden_grad = got_g.transpose(1, 2, 0, 3).reshape(tok, top, units)
    hg32 = hidden_grad.astype(F32)
    weight_grad = jnp.sum(hg32 * hidden.astype(F32), axis=-1).astype(BF16)
    cot = route_weights.astype(F32)[..., None] * hg32
    gate_grad = cot * up * sig * (1.0 + gate * (1.0 - sig))
    up_grad = cot * gate * sig
    pre_grad = jnp.concatenate([gate_grad, up_grad], axis=-1).astype(BF16)
    summed = lax.psum_scatter(
        part.reshape(experts, rows, width).astype(BF16), "expert", scatter_dimension=0, tiled=True
    )
    down_grad = (summed.astype(F32) / ndp).astype(BF16)
    return (pre_grad, weight_grad, down_grad)


def solution(mesh):
    return jax.shard_map(
        body,
        mesh=mesh,
        in_specs=(
            P(("dp", "expert"), None),
            P(("dp", "expert"), None),
            P(("dp", "expert"), None),
            P(("dp", "expert"), None, None),
            P("expert", "dp", None),
        ),
        out_specs=(
            P(("dp", "expert"), None, None),
            P(("dp", "expert"), None),
            P("expert", "dp", None),
        ),
        check_vma=False,
    )
```

profile of v0, /device:TPU:4, one launch (start us, length us, event | category | flops | bytes accessed | tf_op | source)
XLA Modules:
  0.0 325.2 jit_solution(932634305599170821)
XLA Ops:
  7.2 0.7 all-gather.3.cloned.1.call-update
  7.9 0.7 all-gather.5.cloned.1.call-update
  8.6 1.9 fusion.30
  10.6 0.7 copy.37
  11.3 0.7 copy.36
  12.0 24.4 %all_gather.15 = bf16[4096,4]{0,1:T(4,128)(2,1)S(1)} all-gather(bf16[128,4]{0,1:T(4,128)(2,1)S(1)} %copy-done.1), channel_id=1, replica_groups=mesh['dp'=32,'expert'=16] {'dp'}, dimensions={0}, use_global_device_ids=true | all-gather | bytes 33792 | tf_op jit(solution)/shard_map/all_gather | solution.py:11
  36.4 24.9 %all_gather.12 = s32[4096,4]{0,1:T(4,128)S(1)} all-gather(s32[128,4]{0,1:T(4,128)S(1)} %copy-done.2), channel_id=1, replica_groups=mesh['dp'=32,'expert'=16] {'dp'}, dimensions={0}, use_global_device_ids=true | all-gather | bytes 67584 | tf_op jit(solution)/shard_map/all_gather | solution.py:11
  61.5 24.7 %all-gather.3.cloned.1.call-done = bf16[16,24,2048]{2,1,0:T(8,128)(2,1)} async-done(((bf16[1,24,2048]{2,1,0:T(8,128)(2,1)}), bf16[16,24,2048]{2,1,0:T(8,128)(2,1)}) %all-gather.3.cloned.1.call-update) | async-done | bytes 1572880 | tf_op jit(solution)/shard_map/all_gather | solution.py:21
  86.3 88.2 %all-gather.5.cloned.1.call-done = bf16[4096,2048]{1,0:T(8,128)(2,1)} async-done(((bf16[128,2048]{1,0:T(8,128)(2,1)}), bf16[4096,2048]{1,0:T(8,128)(2,1)}) %all-gather.5.cloned.1.call-update) | async-done | bytes 16777232 | tf_op jit(solution)/shard_map/all_gather | solution.py:11
  174.5 12.7 %select_reduce_fusion.3 = (bf16[24,4096]{1,0:T(8,128)(2,1)S(1)}, bf16[24,4096]{1,0:T(8,128)(2,1)S(1)}, bf16[24,4096]{1,0:T(8,128)(2,1)S(1)}, bf16[24,4096]{1,0:T(8,128)(2,1)S(1)}) fusion(pred[16,4096]{1,0:T(8,128)(4,1)S(1)} %get-tuple-element.37, pred[16,4096]{1,0:T(8,128)(4,1)S(1)} %get-tuple-element.34, pred[16,4096]{1,0:T(8,128)(4,1)S(1)} %get-tuple-element.35, ...), kind=kOutput, calls=%fused_computation.8 | convolution fusion | flops 6454640640 | bytes 19398656 | tf_op jit(solution)/shard_map/dot_general | solution.py:42
  187.5 1.2 copy.25
  188.7 5.7 %all-to-all-start = ((bf16[32,128,4,24]{1,3,2,0:T(8,128)(2,1)}), bf16[32,128,4,24]{1,3,2,0:T(8,128)(2,1)S(1)}, u32[]{:S(2)}, u32[]{:S(2)}) async-start(bf16[32,128,4,24]{1,3,2,0:T(8,128)(2,1)} %copy.25), calls=%async_computation | async-start | bytes 1572864 | tf_op jit(solution)/shard_map/all_to_all | solution.py:48
  194.4 12.1 %all-to-all-done = bf16[32,128,4,24]{1,3,2,0:T(8,128)(2,1)S(1)} async-done(((bf16[32,128,4,24]{1,3,2,0:T(8,128)(2,1)}), bf16[32,128,4,24]{1,3,2,0:T(8,128)(2,1)S(1)}, u32[]{:S(2)}, u32[]{:S(2)}) %all-to-all-start) | async-done | bytes 786464 | tf_op jit(solution)/shard_map/all_to_all | solution.py:48
  206.5 2.6 fusion.26
  209.1 1.0 copy.29
  210.1 5.9 %all-to-all-start.1 = ((bf16[32,128,4,24]{1,3,2,0:T(8,128)(2,1)}), bf16[32,128,4,24]{1,3,2,0:T(8,128)(2,1)S(1)}, u32[]{:S(2)}, u32[]{:S(2)}) async-start(bf16[32,128,4,24]{1,3,2,0:T(8,128)(2,1)} %copy.29), calls=%async_computation.1 | async-start | bytes 1572864 | tf_op jit(solution)/shard_map/all_to_all | solution.py:32
  216.0 0.2 reduce-scatter.2.cloned.1.call-start
  216.3 11.8 %all-to-all-done.1 = bf16[32,128,4,24]{1,3,2,0:T(8,128)(2,1)S(1)} async-done(((bf16[32,128,4,24]{1,3,2,0:T(8,128)(2,1)}), bf16[32,128,4,24]{1,3,2,0:T(8,128)(2,1)S(1)}, u32[]{:S(2)}, u32[]{:S(2)}) %all-to-all-start.1) | async-done | bytes 786464 | tf_op jit(solution)/shard_map/all_to_all | solution.py:32
  228.1 0.3 convert_bitcast_fusion
  228.5 0.3 broadcast_multiply_fusion
  228.8 0.2 copy.50
  229.1 0.3 broadcast_multiply_fusion.1
  229.4 0.2 copy.51
  229.6 0.3 broadcast_multiply_fusion.2
  229.9 0.2 copy.52
  230.2 0.3 broadcast_multiply_fusion.3
  230.5 0.2 copy.53
  230.8 13.7 %fusion.13 = bf16[16,24,2048]{2,1,0:T(8,128)(2,1)} fusion(bf16[4096,2048]{1,0:T(8,128)(2,1)} %all-gather.5.cloned.1.call-done, f32[24,4096]{1,0:T(8,128)S(1)} %bitcast.84, f32[24,4096]{1,0:T(8,128)S(1)} %bitcast.85, f32[24,4096]{1,0:T(8,128)S(1)} %bitcast.86, f32[24,4096]{1,0:T(8,128)S(1)} %bitcast.87, pred[16,4096]{1,0:T(8,128)(4,1)S(1)} %get-tuple-element.34, ...), kind=kOutput, calls=%fused_computation.18 | convolution fusion | flops 6455820288 | bytes 20185088 | tf_op jit(solution)/shard_map/dot_general | solution.py:41
  244.5 1.1 copy-done
  245.7 2.5 copy.31
  248.2 69.0 %reduce-scatter.2.cloned.1.call-done = bf16[1,24,2048]{2,1,0:T(8,128)(2,1)} async-done(((bf16[16,24,2048]{2,1,0:T(8,128)(2,1)}), bf16[1,24,2048]{2,1,0:T(8,128)(2,1)}) %reduce-scatter.2.cloned.1.call-update) | async-done | bytes 98320 | tf_op jit(solution)/shard_map/reduce_scatter | solution.py:56
  317.1 1.6 multiply_convert_fusion
  (21 shorter events, 0.8 us)
Async XLA Ops:
  7.2 79.1 %all-gather.3.cloned.1.call-start = ((), (), s32[]{:S(2)}) async-start(), calls=%async_computation.3 | async-start | bytes 1671168 | tf_op jit(solution)/shard_map/all_gather | solution.py:21
  7.9 166.6 %all-gather.5.cloned.1.call-start = ((), (), s32[]{:S(2)}) async-start(), calls=%async_computation.4 | async-start | bytes 17301504 | tf_op jit(solution)/shard_map/all_gather | solution.py:11
  10.6 1.4 copy-start.1
  10.6 25.8 %copy-start.2 = (s32[128,4]{0,1:T(4,128)S(1)}, s32[128,4]{0,1:T(4,128)}, u32[]{:S(2)}) copy-start(s32[128,4]{0,1:T(4,128)} %param.6) | copy-start | bytes 6148
  188.7 17.8 %all-to-all-start = ((bf16[32,128,4,24]{1,3,2,0:T(8,128)(2,1)}), bf16[32,128,4,24]{1,3,2,0:T(8,128)(2,1)S(1)}, u32[]{:S(2)}, u32[]{:S(2)}) async-start(bf16[32,128,4,24]{1,3,2,0:T(8,128)(2,1)} %copy.25), calls=%async_computation | async-start | bytes 1572864 | tf_op jit(solution)/shard_map/all_to_all | solution.py:48
  210.1 18.0 %all-to-all-start.1 = ((bf16[32,128,4,24]{1,3,2,0:T(8,128)(2,1)}), bf16[32,128,4,24]{1,3,2,0:T(8,128)(2,1)S(1)}, u32[]{:S(2)}, u32[]{:S(2)}) async-start(bf16[32,128,4,24]{1,3,2,0:T(8,128)(2,1)} %copy.29), calls=%async_computation.1 | async-start | bytes 1572864 | tf_op jit(solution)/shard_map/all_to_all | solution.py:32
  216.0 101.1 %reduce-scatter.2.cloned.1.call-start = ((), (), s32[]{:S(2)}) async-start(), calls=%async_computation.5 | async-start | bytes 1671168 | tf_op jit(solution)/shard_map/reduce_scatter | solution.py:56
  244.4 1.1 copy-start
Sparse Core Ops, SparseCore 0:
  10.1 76.1 all-gather.2
  89.4 85.0 all-gather.4
  244.6 72.4 reduce-scatter.1
where the time goes:
time: 326 us; the launch traced here: 325 us
  waiting for transfers between devices  207 us (63%)
  blocking collectives  49.4 us (15%)
  matrix products  26.4 us (8%)
  between operations  14 us (4%)
  starting transfers between devices  11.9 us (4%)
  local copies, waits for them, and re-layouts  10.3 us (3%)
  other arithmetic  6.07 us (2%)
    all_gather x1, waiting for transfers between devices, gather_rows(): return lax.all_gather(x, 'dp', axis=0, tiled=True)  88.2 us
    reduce_scatter x1, waiting for transfers between devices, body(): lax.psum_scatter(part.reshape(experts, rows, width).astype(BF16), 'expert...  69 us
    all_gather x2, blocking collectives, gather_rows(): return lax.all_gather(x, 'dp', axis=0, tiled=True)  49.4 us
    all_gather x1, waiting for transfers between devices, body(): w_all = lax.all_gather(down_weight, 'expert', axis=0, tiled=True)  24.7 us
    dot_general x1, matrix products, body(): lax.dot_general(hp, og_all, (((1,), (0,)), ((), ())), preferred_element_t...  13.7 us
    dot_general x1, matrix products, body(): lax.dot_general(wcat, og_all, (((1,), (1,)), ((), ())), preferred_element...  12.7 us
    all_to_all x1, waiting for transfers between devices, body(): got_g = lax.all_to_all(send_g, 'dp', 0, 0, tiled=True)  12.1 us
    all_to_all x1, waiting for transfers between devices, body(): got_h = lax.all_to_all(send_h, 'dp', 0, 0, tiled=True)  11.8 us
  transfers between devices with their start and end apart: 5, of which 5 were waited for; matrix products, arithmetic and copies ran while one was open for 2% of the time, Pallas kernels for 0%

commit v1 on v0

--- a/solution.py
+++ b/solution.py
@@ -18,7 +18,26 @@
     ndp = lax.axis_size("dp")
     rows = down_weight.shape[1]
     n_all = ndp * tok
-    w_all = lax.all_gather(down_weight, "expert", axis=0, tiled=True)
+    size, index, width_2 = (lax.axis_size("expert"), lax.axis_index("expert"), down_weight.shape[0])
+    ahead = [(i, (i + 1) % size) for i in range(size)]
+    behind = [(i, (i - 1) % size) for i in range(size)]
+    whole = jnp.zeros(
+        (*down_weight.shape[:0], size * width_2, *down_weight.shape[0 + 1 :]), down_weight.dtype
+    )
+    whole = lax.dynamic_update_slice_in_dim(whole, down_weight, index * width_2, axis=0)
+    from_left = from_right = down_weight
+    middle = size // 2
+    for hop in range(1, middle + 1):
+        from_left = lax.ppermute(from_left, "expert", ahead)
+        whole = lax.dynamic_update_slice_in_dim(
+            whole, from_left, (index - hop) % size * width_2, axis=0
+        )
+        if hop < size - middle:
+            from_right = lax.ppermute(from_right, "expert", behind)
+            whole = lax.dynamic_update_slice_in_dim(
+                whole, from_right, (index + hop) % size * width_2, axis=0
+            )
+    w_all = whole
     experts = w_all.shape[0]
     wcat = w_all.reshape(experts * rows, width)
     og_all = gather_rows(out_grad)

time: 326 us -> 281 us (0.86)
  the two profiles are of different devices: /device:TPU:4 before, /device:TPU:2 now
where the time goes in v1:
time: 281 us; the launch traced here: 280 us
  waiting for transfers between devices  94.6 us (34%)
  starting transfers between devices  70.1 us (25%)
  blocking collectives  46.7 us (17%)
  matrix products  26.3 us (9%)
  local copies, waits for them, and re-layouts  22 us (8%)
  between operations  14.6 us (5%)
  other arithmetic  6.06 us (2%)
    reduce_scatter x1, waiting for transfers between devices, body(): lax.psum_scatter(part.reshape(experts, rows, width).astype(BF16), 'expert...  65.6 us
    all_gather x2, blocking collectives, gather_rows(): return lax.all_gather(x, 'dp', axis=0, tiled=True)  46.7 us
    ppermute x7, starting transfers between devices, body(): from_right = lax.ppermute(from_right, 'expert', behind)  40.3 us
    ppermute x8, starting transfers between devices, body(): from_left = lax.ppermute(from_left, 'expert', ahead)  17.2 us
    dot_general x1, matrix products, body(): lax.dot_general(hp, og_all, (((1,), (0,)), ((), ())), preferred_element_t...  13.6 us
    dot_general x1, matrix products, body(): lax.dot_general(wcat, og_all, (((1,), (1,)), ((), ())), preferred_element...  12.7 us
    all_to_all x1, waiting for transfers between devices, body(): got_g = lax.all_to_all(send_g, 'dp', 0, 0, tiled=True)  12 us
    all_to_all x1, waiting for transfers between devices, body(): got_h = lax.all_to_all(send_h, 'dp', 0, 0, tiled=True)  11.8 us
  transfers between devices with their start and end apart: 19, of which 4 were waited for; matrix products, arithmetic and copies ran while one was open for 6% of the time, Pallas kernels for 0%

profile of v1, /device:TPU:2, one launch (start us, length us, event | category | flops | bytes accessed | tf_op | source)
XLA Modules:
  0.0 280.5 jit_solution(1505820887417585490)
XLA Ops:
  7.9 3.8 %collective-permute-start = (bf16[1,24,2048]{2,1,0:T(8,128)(2,1)}, bf16[1,24,2048]{2,1,0:T(8,128)(2,1)S(1)}, u32[]{:S(2)}, u32[]{:S(2)}) collective-permute-start(bf16[1,24,2048]{2,1,0:T(8,128)(2,1)} %param.9), channel_id=1, source_target_pairs={{0,1},{1,2},{2,3},{3,4},{4,5},{5,6},{6,7},{7,8},{8,9},{9,10},{10,1... | collective-permute-start | bytes 294920 | tf_op jit(solution)/shard_map/ppermute | solution.py:31
  11.7 9.5 %collective-permute-start.1 = (bf16[1,24,2048]{2,1,0:T(8,128)(2,1)}, bf16[1,24,2048]{2,1,0:T(8,128)(2,1)S(1)}, u32[]{:S(2)}, u32[]{:S(2)}) collective-permute-start(bf16[1,24,2048]{2,1,0:T(8,128)(2,1)} %param.9), channel_id=1, source_target_pairs={{0,15},{1,0},{2,1},{3,2},{4,3},{5,4},{6,5},{7,6},{8,7},{9,8},{10,9... | collective-permute-start | bytes 294920 | tf_op jit(solution)/shard_map/ppermute | solution.py:36
  21.2 24.3 %all_gather.9 = s32[4096,4]{0,1:T(4,128)S(1)} all-gather(s32[128,4]{0,1:T(4,128)} %param.6), channel_id=1, replica_groups=mesh['dp'=32,'expert'=16] {'dp'}, dimensions={0}, use_global_device_ids=true | all-gather | bytes 67584 | tf_op jit(solution)/shard_map/all_gather | solution.py:11
  45.5 1.9 fusion.30
  47.7 1.3 broadcast_in_dim.91
  51.1 22.5 %all_gather.11 = bf16[4096,4]{0,1:T(4,128)(2,1)S(1)} all-gather(bf16[128,4]{0,1:T(4,128)(2,1)S(1)} %copy-done.4), channel_id=1, replica_groups=mesh['dp'=32,'expert'=16] {'dp'}, dimensions={0}, use_global_device_ids=true | all-gather | bytes 33792 | tf_op jit(solution)/shard_map/all_gather | solution.py:11
  73.6 1.9 collective-permute-start.2
  75.5 5.1 %collective-permute-start.3 = (bf16[1,24,2048]{2,1,0:T(8,128)(2,1)S(1)}, bf16[1,24,2048]{2,1,0:T(8,128)(2,1)S(1)}, u32[]{:S(2)}, u32[]{:S(2)}) collective-permute-start(bf16[1,24,2048]{2,1,0:T(8,128)(2,1)S(1)} %collective-permute-done.1), channel_id=1, source_target_pairs={{0,15},{1,0},{2,1},{3,2},{4,3},{5,4},{6,5},{7,6},{8,7},{9,8},{10,9... | collective-permute-start | bytes 294920 | tf_op jit(solution)/shard_map/ppermute | solution.py:36
  81.9 1.9 collective-permute-start.4
  83.9 5.1 %collective-permute-start.5 = (bf16[1,24,2048]{2,1,0:T(8,128)(2,1)S(1)}, bf16[1,24,2048]{2,1,0:T(8,128)(2,1)S(1)}, u32[]{:S(2)}, u32[]{:S(2)}) collective-permute-start(bf16[1,24,2048]{2,1,0:T(8,128)(2,1)S(1)} %collective-permute-done.3), channel_id=1, source_target_pairs={{0,15},{1,0},{2,1},{3,2},{4,3},{5,4},{6,5},{7,6},{8,7},{9,8},{10,9... | collective-permute-start | bytes 294920 | tf_op jit(solution)/shard_map/ppermute | solution.py:36
  90.3 1.9 collective-permute-start.6
  92.2 5.1 %collective-permute-start.7 = (bf16[1,24,2048]{2,1,0:T(8,128)(2,1)S(1)}, bf16[1,24,2048]{2,1,0:T(8,128)(2,1)S(1)}, u32[]{:S(2)}, u32[]{:S(2)}) collective-permute-start(bf16[1,24,2048]{2,1,0:T(8,128)(2,1)S(1)} %collective-permute-done.5), channel_id=1, source_target_pairs={{0,15},{1,0},{2,1},{3,2},{4,3},{5,4},{6,5},{7,6},{8,7},{9,8},{10,9... | collective-permute-start | bytes 294920 | tf_op jit(solution)/shard_map/ppermute | solution.py:36
  98.7 1.9 collective-permute-start.8
  100.6 5.1 %collective-permute-start.9 = (bf16[1,24,2048]{2,1,0:T(8,128)(2,1)S(1)}, bf16[1,24,2048]{2,1,0:T(8,128)(2,1)S(1)}, u32[]{:S(2)}, u32[]{:S(2)}) collective-permute-start(bf16[1,24,2048]{2,1,0:T(8,128)(2,1)S(1)} %collective-permute-done.7), channel_id=1, source_target_pairs={{0,15},{1,0},{2,1},{3,2},{4,3},{5,4},{6,5},{7,6},{8,7},{9,8},{10,9... | collective-permute-start | bytes 294920 | tf_op jit(solution)/shard_map/ppermute | solution.py:36
  107.1 1.9 collective-permute-start.10
  109.0 5.1 %collective-permute-start.11 = (bf16[1,24,2048]{2,1,0:T(8,128)(2,1)S(1)}, bf16[1,24,2048]{2,1,0:T(8,128)(2,1)S(1)}, u32[]{:S(2)}, u32[]{:S(2)}) collective-permute-start(bf16[1,24,2048]{2,1,0:T(8,128)(2,1)S(1)} %collective-permute-done.9), channel_id=1, source_target_pairs={{0,15},{1,0},{2,1},{3,2},{4,3},{5,4},{6,5},{7,6},{8,7},{9,8},{10,9... | collective-permute-start | bytes 294920 | tf_op jit(solution)/shard_map/ppermute | solution.py:36
  115.4 1.9 collective-permute-start.12
  117.4 5.1 %collective-permute-start.13 = (bf16[1,24,2048]{2,1,0:T(8,128)(2,1)S(1)}, bf16[1,24,2048]{2,1,0:T(8,128)(2,1)S(1)}, u32[]{:S(2)}, u32[]{:S(2)}) collective-permute-start(bf16[1,24,2048]{2,1,0:T(8,128)(2,1)S(1)} %collective-permute-done.11), channel_id=1, source_target_pairs={{0,15},{1,0},{2,1},{3,2},{4,3},{5,4},{6,5},{7,6},{8,7},{9,8},{10,9... | collective-permute-start | bytes 294920 | tf_op jit(solution)/shard_map/ppermute | solution.py:36
  123.8 1.9 collective-permute-start.14
  127.0 4.5 %collective-permute-done.14 = bf16[1,24,2048]{2,1,0:T(8,128)(2,1)S(1)} collective-permute-done((bf16[1,24,2048]{2,1,0:T(8,128)(2,1)S(1)}, bf16[1,24,2048]{2,1,0:T(8,128)(2,1)S(1)}, u32[]{:S(2)}, u32[]{:S(2)}) %collective-permute-start.14) | collective-permute-done | bytes 98336 | tf_op jit(solution)/shard_map/ppermute | solution.py:31
  132.2 12.7 %select_reduce_fusion.3 = (bf16[24,4096]{1,0:T(8,128)(2,1)S(1)}, bf16[24,4096]{1,0:T(8,128)(2,1)S(1)}, bf16[24,4096]{1,0:T(8,128)(2,1)S(1)}, bf16[24,4096]{1,0:T(8,128)(2,1)S(1)}) fusion(pred[16,4096]{1,0:T(8,128)(4,1)S(1)} %get-tuple-element.37, pred[16,4096]{1,0:T(8,128)(4,1)S(1)} %get-tuple-element.34, pred[16,4096]{1,0:T(8,128)(4,1)S(1)} %get-tuple-element.35, ...), kind=kOutput, calls=%fused_computation.8 | convolution fusion | flops 6454640640 | bytes 19398656 | tf_op jit(solution)/shard_map/dot_general | solution.py:61
  145.2 1.2 copy.25
  146.4 6.4 %all-to-all-start = ((bf16[32,128,4,24]{1,3,2,0:T(8,128)(2,1)}), bf16[32,128,4,24]{1,3,2,0:T(8,128)(2,1)S(1)}, u32[]{:S(2)}, u32[]{:S(2)}) async-start(bf16[32,128,4,24]{1,3,2,0:T(8,128)(2,1)} %copy.25), calls=%async_computation | async-start | bytes 1572864 | tf_op jit(solution)/shard_map/all_to_all | solution.py:67
  152.8 12.0 %all-to-all-done = bf16[32,128,4,24]{1,3,2,0:T(8,128)(2,1)S(1)} async-done(((bf16[32,128,4,24]{1,3,2,0:T(8,128)(2,1)}), bf16[32,128,4,24]{1,3,2,0:T(8,128)(2,1)S(1)}, u32[]{:S(2)}, u32[]{:S(2)}) %all-to-all-start) | async-done | bytes 786464 | tf_op jit(solution)/shard_map/all_to_all | solution.py:67
  164.8 2.6 fusion.26
  168.4 6.0 %all-to-all-start.1 = ((bf16[32,128,4,24]{1,3,2,0:T(8,128)(2,1)}), bf16[32,128,4,24]{1,3,2,0:T(8,128)(2,1)S(1)}, u32[]{:S(2)}, u32[]{:S(2)}) async-start(bf16[32,128,4,24]{1,3,2,0:T(8,128)(2,1)} %copy.29), calls=%async_computation.1 | async-start | bytes 1572864 | tf_op jit(solution)/shard_map/all_to_all | solution.py:51
  174.7 11.8 %all-to-all-done.1 = bf16[32,128,4,24]{1,3,2,0:T(8,128)(2,1)S(1)} async-done(((bf16[32,128,4,24]{1,3,2,0:T(8,128)(2,1)}), bf16[32,128,4,24]{1,3,2,0:T(8,128)(2,1)S(1)}, u32[]{:S(2)}, u32[]{:S(2)}) %all-to-all-start.1) | async-done | bytes 786464 | tf_op jit(solution)/shard_map/all_to_all | solution.py:51
  189.2 13.6 %fusion.13 = bf16[16,24,2048]{2,1,0:T(8,128)(2,1)} fusion(bf16[4096,2048]{1,0:T(8,128)(2,1)} %all-gather.2.cloned.1.call-done, f32[24,4096]{1,0:T(8,128)S(1)} %bitcast.84, f32[24,4096]{1,0:T(8,128)S(1)} %bitcast.85, f32[24,4096]{1,0:T(8,128)S(1)} %bitcast.86, f32[24,4096]{1,0:T(8,128)S(1)} %bitcast.87, pred[16,4096]{1,0:T(8,128)(4,1)S(1)} %get-tuple-element.34, ...), kind=kOutput, calls=%fused_computation.18 | convolution fusion | flops 6455820288 | bytes 20185088 | tf_op jit(solution)/shard_map/dot_general | solution.py:60
  202.8 1.1 copy-done
  204.0 2.5 copy.31
  206.5 65.6 %reduce-scatter.2.cloned.1.call-done = bf16[1,24,2048]{2,1,0:T(8,128)(2,1)} async-done(((bf16[16,24,2048]{2,1,0:T(8,128)(2,1)}), bf16[1,24,2048]{2,1,0:T(8,128)(2,1)}) %reduce-scatter.2.cloned.1.call-update) | async-done | bytes 98320 | tf_op jit(solution)/shard_map/reduce_scatter | solution.py:75
  272.1 1.6 multiply_convert_fusion
  (69 shorter events, 16.9 us)
Async XLA Ops:
  7.2 125.0 %all-gather.2.cloned.1.call-start = ((), (), s32[]{:S(2)}) async-start(), calls=%async_computation.3 | async-start | bytes 17301504 | tf_op jit(solution)/shard_map/all_gather | solution.py:11
  7.9 65.7 %collective-permute-start = (bf16[1,24,2048]{2,1,0:T(8,128)(2,1)}, bf16[1,24,2048]{2,1,0:T(8,128)(2,1)S(1)}, u32[]{:S(2)}, u32[]{:S(2)}) collective-permute-start(bf16[1,24,2048]{2,1,0:T(8,128)(2,1)} %param.9), channel_id=1, source_target_pairs={{0,1},{1,2},{2,3},{3,4},{4,5},{5,6},{6,7},{7,8},{8,9},{9,10},{10,1... | collective-permute-start | bytes 294920 | tf_op jit(solution)/shard_map/ppermute | solution.py:31
  11.7 63.8 %collective-permute-start.1 = (bf16[1,24,2048]{2,1,0:T(8,128)(2,1)}, bf16[1,24,2048]{2,1,0:T(8,128)(2,1)S(1)}, u32[]{:S(2)}, u32[]{:S(2)}) collective-permute-start(bf16[1,24,2048]{2,1,0:T(8,128)(2,1)} %param.9), channel_id=1, source_target_pairs={{0,15},{1,0},{2,1},{3,2},{4,3},{5,4},{6,5},{7,6},{8,7},{9,8},{10,9... | collective-permute-start | bytes 294920 | tf_op jit(solution)/shard_map/ppermute | solution.py:36
  47.4 1.6 copy-start.1
  47.7 84.5 %copy-start.2 = (pred[16,4096]{1,0:T(8,128)(4,1)}, pred[16,4096]{1,0:T(8,128)(4,1)S(1)}, u32[]{:S(2)}) copy-start(pred[16,4096]{1,0:T(8,128)(4,1)S(1)} %get-tuple-element.35) | copy-start | bytes 196612
  49.7 1.3 copy-start.4
  73.6 8.4 %collective-permute-start.2 = (bf16[1,24,2048]{2,1,0:T(8,128)(2,1)S(1)}, bf16[1,24,2048]{2,1,0:T(8,128)(2,1)S(1)}, u32[]{:S(2)}, u32[]{:S(2)}) collective-permute-start(bf16[1,24,2048]{2,1,0:T(8,128)(2,1)S(1)} %collective-permute-done), channel_id=1, source_target_pairs={{0,1},{1,2},{2,3},{3,4},{4,5},{5,6},{6,7},{7,8},{8,9},{9,10},{10,1... | collective-permute-start | bytes 294920 | tf_op jit(solution)/shard_map/ppermute | solution.py:31
  75.5 8.4 %collective-permute-start.3 = (bf16[1,24,2048]{2,1,0:T(8,128)(2,1)S(1)}, bf16[1,24,2048]{2,1,0:T(8,128)(2,1)S(1)}, u32[]{:S(2)}, u32[]{:S(2)}) collective-permute-start(bf16[1,24,2048]{2,1,0:T(8,128)(2,1)S(1)} %collective-permute-done.1), channel_id=1, source_target_pairs={{0,15},{1,0},{2,1},{3,2},{4,3},{5,4},{6,5},{7,6},{8,7},{9,8},{10,9... | collective-permute-start | bytes 294920 | tf_op jit(solution)/shard_map/ppermute | solution.py:36
  81.9 8.4 %collective-permute-start.4 = (bf16[1,24,2048]{2,1,0:T(8,128)(2,1)S(1)}, bf16[1,24,2048]{2,1,0:T(8,128)(2,1)S(1)}, u32[]{:S(2)}, u32[]{:S(2)}) collective-permute-start(bf16[1,24,2048]{2,1,0:T(8,128)(2,1)S(1)} %collective-permute-done.2), channel_id=1, source_target_pairs={{0,1},{1,2},{2,3},{3,4},{4,5},{5,6},{6,7},{7,8},{8,9},{9,10},{10,1... | collective-permute-start | bytes 294920 | tf_op jit(solution)/shard_map/ppermute | solution.py:31
  83.9 8.4 %collective-permute-start.5 = (bf16[1,24,2048]{2,1,0:T(8,128)(2,1)S(1)}, bf16[1,24,2048]{2,1,0:T(8,128)(2,1)S(1)}, u32[]{:S(2)}, u32[]{:S(2)}) collective-permute-start(bf16[1,24,2048]{2,1,0:T(8,128)(2,1)S(1)} %collective-permute-done.3), channel_id=1, source_target_pairs={{0,15},{1,0},{2,1},{3,2},{4,3},{5,4},{6,5},{7,6},{8,7},{9,8},{10,9... | collective-permute-start | bytes 294920 | tf_op jit(solution)/shard_map/ppermute | solution.py:36
  90.3 8.4 %collective-permute-start.6 = (bf16[1,24,2048]{2,1,0:T(8,128)(2,1)S(1)}, bf16[1,24,2048]{2,1,0:T(8,128)(2,1)S(1)}, u32[]{:S(2)}, u32[]{:S(2)}) collective-permute-start(bf16[1,24,2048]{2,1,0:T(8,128)(2,1)S(1)} %collective-permute-done.4), channel_id=1, source_target_pairs={{0,1},{1,2},{2,3},{3,4},{4,5},{5,6},{6,7},{7,8},{8,9},{9,10},{10,1... | collective-permute-start | bytes 294920 | tf_op jit(solution)/shard_map/ppermute | solution.py:31
  92.2 8.4 %collective-permute-start.7 = (bf16[1,24,2048]{2,1,0:T(8,128)(2,1)S(1)}, bf16[1,24,2048]{2,1,0:T(8,128)(2,1)S(1)}, u32[]{:S(2)}, u32[]{:S(2)}) collective-permute-start(bf16[1,24,2048]{2,1,0:T(8,128)(2,1)S(1)} %collective-permute-done.5), channel_id=1, source_target_pairs={{0,15},{1,0},{2,1},{3,2},{4,3},{5,4},{6,5},{7,6},{8,7},{9,8},{10,9... | collective-permute-start | bytes 294920 | tf_op jit(solution)/shard_map/ppermute | solution.py:36
  98.7 8.4 %collective-permute-start.8 = (bf16[1,24,2048]{2,1,0:T(8,128)(2,1)S(1)}, bf16[1,24,2048]{2,1,0:T(8,128)(2,1)S(1)}, u32[]{:S(2)}, u32[]{:S(2)}) collective-permute-start(bf16[1,24,2048]{2,1,0:T(8,128)(2,1)S(1)} %collective-permute-done.6), channel_id=1, source_target_pairs={{0,1},{1,2},{2,3},{3,4},{4,5},{5,6},{6,7},{7,8},{8,9},{9,10},{10,1... | collective-permute-start | bytes 294920 | tf_op jit(solution)/shard_map/ppermute | solution.py:31
  100.6 8.4 %collective-permute-start.9 = (bf16[1,24,2048]{2,1,0:T(8,128)(2,1)S(1)}, bf16[1,24,2048]{2,1,0:T(8,128)(2,1)S(1)}, u32[]{:S(2)}, u32[]{:S(2)}) collective-permute-start(bf16[1,24,2048]{2,1,0:T(8,128)(2,1)S(1)} %collective-permute-done.7), channel_id=1, source_target_pairs={{0,15},{1,0},{2,1},{3,2},{4,3},{5,4},{6,5},{7,6},{8,7},{9,8},{10,9... | collective-permute-start | bytes 294920 | tf_op jit(solution)/shard_map/ppermute | solution.py:36
  107.1 8.4 %collective-permute-start.10 = (bf16[1,24,2048]{2,1,0:T(8,128)(2,1)S(1)}, bf16[1,24,2048]{2,1,0:T(8,128)(2,1)S(1)}, u32[]{:S(2)}, u32[]{:S(2)}) collective-permute-start(bf16[1,24,2048]{2,1,0:T(8,128)(2,1)S(1)} %collective-permute-done.8), channel_id=1, source_target_pairs={{0,1},{1,2},{2,3},{3,4},{4,5},{5,6},{6,7},{7,8},{8,9},{9,10},{10,1... | collective-permute-start | bytes 294920 | tf_op jit(solution)/shard_map/ppermute | solution.py:31
  109.0 8.4 %collective-permute-start.11 = (bf16[1,24,2048]{2,1,0:T(8,128)(2,1)S(1)}, bf16[1,24,2048]{2,1,0:T(8,128)(2,1)S(1)}, u32[]{:S(2)}, u32[]{:S(2)}) collective-permute-start(bf16[1,24,2048]{2,1,0:T(8,128)(2,1)S(1)} %collective-permute-done.9), channel_id=1, source_target_pairs={{0,15},{1,0},{2,1},{3,2},{4,3},{5,4},{6,5},{7,6},{8,7},{9,8},{10,9... | collective-permute-start | bytes 294920 | tf_op jit(solution)/shard_map/ppermute | solution.py:36
  115.4 8.4 %collective-permute-start.12 = (bf16[1,24,2048]{2,1,0:T(8,128)(2,1)S(1)}, bf16[1,24,2048]{2,1,0:T(8,128)(2,1)S(1)}, u32[]{:S(2)}, u32[]{:S(2)}) collective-permute-start(bf16[1,24,2048]{2,1,0:T(8,128)(2,1)S(1)} %collective-permute-done.10), channel_id=1, source_target_pairs={{0,1},{1,2},{2,3},{3,4},{4,5},{5,6},{6,7},{7,8},{8,9},{9,10},{10,1... | collective-permute-start | bytes 294920 | tf_op jit(solution)/shard_map/ppermute | solution.py:31
  117.4 9.0 %collective-permute-start.13 = (bf16[1,24,2048]{2,1,0:T(8,128)(2,1)S(1)}, bf16[1,24,2048]{2,1,0:T(8,128)(2,1)S(1)}, u32[]{:S(2)}, u32[]{:S(2)}) collective-permute-start(bf16[1,24,2048]{2,1,0:T(8,128)(2,1)S(1)} %collective-permute-done.11), channel_id=1, source_target_pairs={{0,15},{1,0},{2,1},{3,2},{4,3},{5,4},{6,5},{7,6},{8,7},{9,8},{10,9... | collective-permute-start | bytes 294920 | tf_op jit(solution)/shard_map/ppermute | solution.py:36
  123.8 7.7 %collective-permute-start.14 = (bf16[1,24,2048]{2,1,0:T(8,128)(2,1)S(1)}, bf16[1,24,2048]{2,1,0:T(8,128)(2,1)S(1)}, u32[]{:S(2)}, u32[]{:S(2)}) collective-permute-start(bf16[1,24,2048]{2,1,0:T(8,128)(2,1)S(1)} %collective-permute-done.12), channel_id=1, source_target_pairs={{0,1},{1,2},{2,3},{3,4},{4,5},{5,6},{6,7},{7,8},{8,9},{9,10},{10,1... | collective-permute-start | bytes 294920 | tf_op jit(solution)/shard_map/ppermute | solution.py:31
  146.4 18.5 %all-to-all-start = ((bf16[32,128,4,24]{1,3,2,0:T(8,128)(2,1)}), bf16[32,128,4,24]{1,3,2,0:T(8,128)(2,1)S(1)}, u32[]{:S(2)}, u32[]{:S(2)}) async-start(bf16[32,128,4,24]{1,3,2,0:T(8,128)(2,1)} %copy.25), calls=%async_computation | async-start | bytes 1572864 | tf_op jit(solution)/shard_map/all_to_all | solution.py:67
  168.4 18.0 %all-to-all-start.1 = ((bf16[32,128,4,24]{1,3,2,0:T(8,128)(2,1)}), bf16[32,128,4,24]{1,3,2,0:T(8,128)(2,1)S(1)}, u32[]{:S(2)}, u32[]{:S(2)}) async-start(bf16[32,128,4,24]{1,3,2,0:T(8,128)(2,1)} %copy.29), calls=%async_computation.1 | async-start | bytes 1572864 | tf_op jit(solution)/shard_map/all_to_all | solution.py:51
  174.4 97.7 %reduce-scatter.2.cloned.1.call-start = ((), (), s32[]{:S(2)}) async-start(), calls=%async_computation.4 | async-start | bytes 1671168 | tf_op jit(solution)/shard_map/reduce_scatter | solution.py:75
  188.0 1.1 copy-start.3
  202.7 1.1 copy-start
Sparse Core Ops, SparseCore 0:
  11.1 92.3 all-gather.1
  202.9 69.1 reduce-scatter.1
